TPU v7x, 512 devices: a whole 4x4x16 slice. The times are simulated.
512 devices in a mesh: cand: 8 (over y, core), doc: 64 (over z, x).
Axes of the slice: x: 4, y: 4, z: 16, core: 2. Of those that a mesh axis runs over, the one named last changes fastest.
Arguments:
- queries: bfloat16 [8192, 8192], P('doc'), may hold values from -6 to 50
- keys_values: bfloat16 [2, 8192, 1024], P(None, 'doc', 'cand'), may hold values from -6 to 50
- factors: float32 [8, 64], P('cand'), may hold values from 1 to 16
- lengths: int32 [16], replicated, may hold values from 1 to 1024, 8192 in all
Outputs:
- attended: bfloat16 [8, 8192, 8192], P('cand', 'doc')
All inputs are finite; a program needn't handle non-finite values.
Results may differ from a plain program's by a relative error of at most 0.0053.
Values may be sent and summed in bfloat16 or wider, within the bound.
No kernel may reach another device: no remote copies, remote signals or barrier semaphores. Data moves between devices by JAX's collectives and lax.ppermute only.
A program may use at most 64 MiB of HBM per device.

v0:
```python
import math
import jax
import jax.numpy as jnp
from jax import lax
from jax.sharding import PartitionSpec as P

H = 64
KVH = 8
HD = 128
SPAN = 8
ROPE_BASE = 500000.0


def passed_along(value, axis, steps):
    count = lax.axis_size(axis)
    first, last = (max(0, -steps), min(count, count - steps))
    return lax.ppermute(value, axis, [(source, source + steps) for source in range(first, last)])


def locate(index_rows, lengths):
    ends = jnp.cumsum(lengths)
    starts = ends - lengths
    docid = jnp.sum((index_rows[:, None] >= ends[None, :]).astype(jnp.int32), axis=1)
    onehot = docid[:, None] == jnp.arange(lengths.shape[0], dtype=jnp.int32)[None, :]
    first_row = jnp.sum(jnp.where(onehot, starts[None, :], 0), axis=1)
    valid = index_rows >= 0
    return (jnp.where(valid, docid, -1), jnp.where(valid, index_rows - first_row, 0))


def rotate(values, offsets, factor):
    row_count = values.shape[0]
    heads_here = values.shape[1] // HD
    half_dim = HD // 2
    shaped = values.reshape(row_count, heads_here, HD).astype(jnp.float32)
    inverse = jnp.power(ROPE_BASE, -2.0 * jnp.arange(half_dim, dtype=jnp.float32) / HD) / factor
    angles = offsets.astype(jnp.float32)[:, None] * inverse[None, :]
    cosine = jnp.cos(angles)[:, None, :]
    sine = jnp.sin(angles)[:, None, :]
    first_half = shaped[..., :half_dim]
    second_half = shaped[..., half_dim:]
    turned = jnp.concatenate(
        [first_half * cosine - second_half * sine, second_half * cosine + first_half * sine],
        axis=-1,
    )
    return turned.reshape(row_count, heads_here * HD).astype(jnp.bfloat16)


def attend(query_rot, key_rot, value_rows, query_doc, query_index, key_doc, key_index):
    row_count = query_rot.shape[0]
    key_count = key_rot.shape[0]
    group_size = H // KVH
    q_grouped = query_rot.reshape(row_count, KVH, group_size, HD).transpose(1, 0, 2, 3)
    k_grouped = key_rot.reshape(key_count, KVH, HD).transpose(1, 0, 2)
    v_grouped = value_rows.reshape(key_count, KVH, HD).transpose(1, 0, 2)
    allowed = (
        (key_doc[None, :] == query_doc[:, None])
        & (key_index[None, :] <= query_index[:, None])
        & (key_doc[None, :] >= 0)
    )
    scale = 1.0 / math.sqrt(HD)

    def per_group(operands):
        q_part, k_part, v_part = operands
        scores = (
            jnp.einsum("rgd,wd->rgw", q_part, k_part, preferred_element_type=jnp.float32) * scale
        )
        scores = jnp.where(allowed[:, None, :], scores, -1e30)
        largest = jnp.max(scores, axis=-1, keepdims=True)
        expw = jnp.exp(scores - largest)
        total = jnp.sum(expw, axis=-1, keepdims=True)
        weights = expw.astype(jnp.bfloat16)
        numer = jnp.einsum("rgw,wd->rgd", weights, v_part, preferred_element_type=jnp.float32)
        return (numer / total).astype(jnp.bfloat16)

    mixed = lax.map(per_group, (q_grouped, k_grouped, v_grouped))
    return mixed.transpose(1, 0, 2, 3).reshape(row_count, H * HD)


def on_device(queries, keys_values, factors, lengths):
    row_count = queries.shape[0]
    device = lax.axis_index("doc")
    query_index = device * row_count + jnp.arange(row_count, dtype=jnp.int32)
    key_index = (device - SPAN) * row_count + jnp.arange((SPAN + 1) * row_count, dtype=jnp.int32)
    whole = lax.all_gather(keys_values, "cand", axis=2, tiled=True)
    pieces = []
    for distance in range(SPAN, 0, -1):
        pieces.append(passed_along(whole, "doc", distance))
    pieces.append(whole)
    window = jnp.concatenate(pieces, axis=1)
    query_doc, query_offset = locate(query_index, lengths)
    key_doc, key_offset = locate(key_index, lengths)
    factor = factors[0]
    query_rot = rotate(queries, query_offset, factor)
    key_rot = rotate(window[0], key_offset, factor)
    mixed = attend(query_rot, key_rot, window[1], query_doc, query_index, key_doc, key_index)
    return mixed[None]


def solution(mesh):
    placed = (P("doc", None), P(None, "doc", "cand"), P("cand", None), P())
    return jax.shard_map(
        on_device, mesh=mesh, in_specs=placed, out_specs=P("cand", "doc", None), check_vma=False
    )
```

profile of v0, /device:TPU:448, one launch (start us, length us, event | category | flops | bytes accessed | tf_op | source)
XLA Modules:
  0.0 222.4 jit_solution(7817300378528015322)
XLA Ops:
  0.0 0.9 copy.19
  1.0 13.6 %all_gather.3 = bf16[2,128,1024]{1,2,0:T(8,128)(2,1)S(1)} all-gather(bf16[2,128,128]{1,2,0:T(8,128)(2,1)S(1)} %copy.19), channel_id=1, replica_groups=mesh['cand'=8,'doc'=64] {'cand'}, dimensions={2}, use_global_device_ids=true | all-gather | bytes 589824 | tf_op jit(solution)/shard_map/all_gather | solution.py:84
  14.6 1.3 collective-permute-start
  15.9 5.1 %collective-permute-start.1 = (bf16[2,128,1024]{1,2,0:T(8,128)(2,1)S(1)}, bf16[2,128,1024]{1,2,0:T(8,128)(2,1)S(1)}, u32[]{:S(2)}, u32[]{:S(2)}) collective-permute-start(bf16[2,128,1024]{1,2,0:T(8,128)(2,1)S(1)} %all_gather.3), channel_id=1, source_target_pairs={{0,7},{1,8},{2,9},{3,10},{4,11},{5,12},{6,13},{7,14},{8,15},{9,16}... | collective-permute-start | bytes 1572872 | tf_op jit(solution)/shard_map/ppermute | solution.py:17
  21.0 1.9 collective-permute-start.2
  22.9 1.9 collective-permute-start.3
  24.9 1.9 collective-permute-start.4
  26.8 2.0 convert_bitcast_fusion
  28.8 0.7 copy.27
  29.6 4.6 %fusion.35 = (f32[128,64,64]{2,1,0:T(8,128)}, f32[128,64,64]{2,1,0:T(8,128)}) fusion(f32[128,64,128]{2,1,0:T(8,128)S(1)} %bitcast.48), kind=kLoop, calls=%fused_computation.60 | loop fusion | bytes 8388608 | tf_op jit(solution)/shard_map/slice | solution.py:39
  34.8 0.3 multiply_cosine_fusion.1
  35.1 8.3 %subtract_convert_fusion = (bf16[128,64,64]{2,0,1:T(8,128)(2,1)S(1)}, bf16[128,64,64]{2,0,1:T(8,128)(2,1)S(1)}) fusion(f32[128,64,64]{2,1,0:T(8,128)} %get-tuple-element.116, f32[128,64,64]{2,1,0:T(8,128)} %get-tuple-element.115, f32[128,64]{1,0:T(8,128)S(1)} %get-tuple-element.120, f32[128,64]{1,0:T(8,128)S(1)} %get-tuple-element.119), kind=kLoop, calls=%fused_computation.23 | loop fusion | flops 4194304 | bytes 6356992 | tf_op jit(solution)/shard_map/convert.4
  43.5 1.1 multiply_cosine_fusion
  44.6 2.5 %pad_maximum_fusion = bf16[128,64,128]{2,0,1:T(8,128)(2,1)} fusion(bf16[128,64,64]{2,0,1:T(8,128)(2,1)S(1)} %get-tuple-element.110, bf16[128,64,64]{2,0,1:T(8,128)(2,1)S(1)} %get-tuple-element.109), kind=kLoop, calls=%fused_computation.27 | loop fusion | flops 4194304 | bytes 4194304 | tf_op jit(solution)/shard_map/concatenate | solution.py:41
  47.1 2.1 collective-permute-start.5
  49.2 1.1 constant_dynamic-update-slice_fusion.8
  50.3 16.4 %collective-permute-done.1 = bf16[2,128,1024]{1,2,0:T(8,128)(2,1)S(1)} collective-permute-done((bf16[2,128,1024]{1,2,0:T(8,128)(2,1)S(1)}, bf16[2,128,1024]{1,2,0:T(8,128)(2,1)S(1)}, u32[]{:S(2)}, u32[]{:S(2)}) %collective-permute-start.1) | collective-permute-done | bytes 524320 | tf_op jit(solution)/shard_map/ppermute | solution.py:17
  66.7 1.9 collective-permute-start.6
  68.7 0.1 constant_dynamic-update-slice_fusion.7
  68.8 22.0 %collective-permute-done.2 = bf16[2,128,1024]{1,2,0:T(8,128)(2,1)S(1)} collective-permute-done((bf16[2,128,1024]{1,2,0:T(8,128)(2,1)S(1)}, bf16[2,128,1024]{1,2,0:T(8,128)(2,1)S(1)}, u32[]{:S(2)}, u32[]{:S(2)}) %collective-permute-start.2) | collective-permute-done | bytes 524320 | tf_op jit(solution)/shard_map/ppermute | solution.py:17
  90.8 1.9 collective-permute-start.7
  92.9 20.1 %collective-permute-done.3 = bf16[2,128,1024]{1,2,0:T(8,128)(2,1)S(1)} collective-permute-done((bf16[2,128,1024]{1,2,0:T(8,128)(2,1)S(1)}, bf16[2,128,1024]{1,2,0:T(8,128)(2,1)S(1)}, u32[]{:S(2)}, u32[]{:S(2)}) %collective-permute-start.3) | collective-permute-done | bytes 524320 | tf_op jit(solution)/shard_map/ppermute | solution.py:17
  113.2 6.8 %collective-permute-done.5 = bf16[2,128,1024]{1,2,0:T(8,128)(2,1)S(1)} collective-permute-done((bf16[2,128,1024]{1,2,0:T(8,128)(2,1)S(1)}, bf16[2,128,1024]{1,2,0:T(8,128)(2,1)S(1)}, u32[]{:S(2)}, u32[]{:S(2)}) %collective-permute-start.5) | collective-permute-done | bytes 524320 | tf_op jit(solution)/shard_map/ppermute | solution.py:17
  120.1 14.6 %collective-permute-done.6 = bf16[2,128,1024]{1,2,0:T(8,128)(2,1)S(1)} collective-permute-done((bf16[2,128,1024]{1,2,0:T(8,128)(2,1)S(1)}, bf16[2,128,1024]{1,2,0:T(8,128)(2,1)S(1)}, u32[]{:S(2)}, u32[]{:S(2)}) %collective-permute-start.6) | collective-permute-done | bytes 524320 | tf_op jit(solution)/shard_map/ppermute | solution.py:17
  134.9 31.8 %collective-permute-done.7 = bf16[2,128,1024]{1,2,0:T(8,128)(2,1)S(1)} collective-permute-done((bf16[2,128,1024]{1,2,0:T(8,128)(2,1)S(1)}, bf16[2,128,1024]{1,2,0:T(8,128)(2,1)S(1)}, u32[]{:S(2)}, u32[]{:S(2)}) %collective-permute-start.7) | collective-permute-done | bytes 524320 | tf_op jit(solution)/shard_map/ppermute | solution.py:17
  166.9 1.8 fusion.34
  168.7 0.3 convert.18
  169.0 0.6 subtract_convert_fusion.1
  169.7 0.2 maximum_bitcast_fusion
  169.9 47.3 %while.11 = (s32[]{:T(128)}, bf16[8,128,8,128]{3,1,2,0:T(8,128)(2,1)}, bf16[8,128,8,128]{3,1,2,0:T(8,128)(2,1)}, bf16[8,1152,128]{1,2,0:T(8,128)(2,1)S(1)}, bf16...) while((s32[]{:T(128)}, ...), condition=%wide.region_8.9_spmd.clone, body=%wide.region_5.8_spmd.clone.sunk | while | flops 613087232 | bytes 15598837 | solution.py:75
  169.9 0.2 and_and_fusion.2
  170.1 2.1 fusion.43
  172.2 1.0 fusion.44
  173.2 2.6 %fusion.45 = bf16[8,128,8,128]{3,1,2,0:T(8,128)(2,1)} fusion(bf16[8,128,8,128]{3,1,2,0:T(8,128)(2,1)} %get-tuple-element.200, s32[]{:T(128)S(6)} %copy.43, f32[128,8,1152]{2,0,1:T(8,128)S(1)} %get-tuple-element.186, f32[128,8]{0,1:T(8,128)S(1)} %get-tuple-element.187, bf16[8,1152,128]{1,2,0:T(8,128)(2,1)} %get-tuple-element.214, ...), kind=kOutput, calls=%fused_computation.11.clone.1 | convolution fusion | flops 304611328 | bytes 5284864 | tf_op jit(solution)/shard_map/while/body/eval_jaxpr/rgw,wd->rgd/dot_general | solution.py:72
  175.8 0.2 and_and_fusion.2
  176.1 2.1 fusion.43
  178.1 1.0 fusion.44
  179.1 2.6 %fusion.45 = bf16[8,128,8,128]{3,1,2,0:T(8,128)(2,1)} fusion(bf16[8,128,8,128]{3,1,2,0:T(8,128)(2,1)} %get-tuple-element.200, s32[]{:T(128)S(6)} %copy.43, f32[128,8,1152]{2,0,1:T(8,128)S(1)} %get-tuple-element.186, f32[128,8]{0,1:T(8,128)S(1)} %get-tuple-element.187, bf16[8,1152,128]{1,2,0:T(8,128)(2,1)} %get-tuple-element.214, ...), kind=kOutput, calls=%fused_computation.11.clone.1 | convolution fusion | flops 304611328 | bytes 5284864 | tf_op jit(solution)/shard_map/while/body/eval_jaxpr/rgw,wd->rgd/dot_general | solution.py:72
  181.7 0.2 and_and_fusion.2
  182.0 2.1 fusion.43
  184.0 1.0 fusion.44
  185.1 2.6 %fusion.45 = bf16[8,128,8,128]{3,1,2,0:T(8,128)(2,1)} fusion(bf16[8,128,8,128]{3,1,2,0:T(8,128)(2,1)} %get-tuple-element.200, s32[]{:T(128)S(6)} %copy.43, f32[128,8,1152]{2,0,1:T(8,128)S(1)} %get-tuple-element.186, f32[128,8]{0,1:T(8,128)S(1)} %get-tuple-element.187, bf16[8,1152,128]{1,2,0:T(8,128)(2,1)} %get-tuple-element.214, ...), kind=kOutput, calls=%fused_computation.11.clone.1 | convolution fusion | flops 304611328 | bytes 5284864 | tf_op jit(solution)/shard_map/while/body/eval_jaxpr/rgw,wd->rgd/dot_general | solution.py:72
  187.7 0.2 and_and_fusion.2
  187.9 2.1 fusion.43
  190.0 1.0 fusion.44
  191.0 2.6 %fusion.45 = bf16[8,128,8,128]{3,1,2,0:T(8,128)(2,1)} fusion(bf16[8,128,8,128]{3,1,2,0:T(8,128)(2,1)} %get-tuple-element.200, s32[]{:T(128)S(6)} %copy.43, f32[128,8,1152]{2,0,1:T(8,128)S(1)} %get-tuple-element.186, f32[128,8]{0,1:T(8,128)S(1)} %get-tuple-element.187, bf16[8,1152,128]{1,2,0:T(8,128)(2,1)} %get-tuple-element.214, ...), kind=kOutput, calls=%fused_computation.11.clone.1 | convolution fusion | flops 304611328 | bytes 5284864 | tf_op jit(solution)/shard_map/while/body/eval_jaxpr/rgw,wd->rgd/dot_general | solution.py:72
  193.6 0.2 and_and_fusion.2
  193.8 2.1 fusion.43
  195.9 1.0 fusion.44
  196.9 2.6 %fusion.45 = bf16[8,128,8,128]{3,1,2,0:T(8,128)(2,1)} fusion(bf16[8,128,8,128]{3,1,2,0:T(8,128)(2,1)} %get-tuple-element.200, s32[]{:T(128)S(6)} %copy.43, f32[128,8,1152]{2,0,1:T(8,128)S(1)} %get-tuple-element.186, f32[128,8]{0,1:T(8,128)S(1)} %get-tuple-element.187, bf16[8,1152,128]{1,2,0:T(8,128)(2,1)} %get-tuple-element.214, ...), kind=kOutput, calls=%fused_computation.11.clone.1 | convolution fusion | flops 304611328 | bytes 5284864 | tf_op jit(solution)/shard_map/while/body/eval_jaxpr/rgw,wd->rgd/dot_general | solution.py:72
  199.5 0.2 and_and_fusion.2
  199.7 2.1 fusion.43
  201.8 1.0 fusion.44
  202.8 2.6 %fusion.45 = bf16[8,128,8,128]{3,1,2,0:T(8,128)(2,1)} fusion(bf16[8,128,8,128]{3,1,2,0:T(8,128)(2,1)} %get-tuple-element.200, s32[]{:T(128)S(6)} %copy.43, f32[128,8,1152]{2,0,1:T(8,128)S(1)} %get-tuple-element.186, f32[128,8]{0,1:T(8,128)S(1)} %get-tuple-element.187, bf16[8,1152,128]{1,2,0:T(8,128)(2,1)} %get-tuple-element.214, ...), kind=kOutput, calls=%fused_computation.11.clone.1 | convolution fusion | flops 304611328 | bytes 5284864 | tf_op jit(solution)/shard_map/while/body/eval_jaxpr/rgw,wd->rgd/dot_general | solution.py:72
  205.4 0.2 and_and_fusion.2
  205.6 2.1 fusion.43
  207.7 1.0 fusion.44
  208.7 2.6 %fusion.45 = bf16[8,128,8,128]{3,1,2,0:T(8,128)(2,1)} fusion(bf16[8,128,8,128]{3,1,2,0:T(8,128)(2,1)} %get-tuple-element.200, s32[]{:T(128)S(6)} %copy.43, f32[128,8,1152]{2,0,1:T(8,128)S(1)} %get-tuple-element.186, f32[128,8]{0,1:T(8,128)S(1)} %get-tuple-element.187, bf16[8,1152,128]{1,2,0:T(8,128)(2,1)} %get-tuple-element.214, ...), kind=kOutput, calls=%fused_computation.11.clone.1 | convolution fusion | flops 304611328 | bytes 5284864 | tf_op jit(solution)/shard_map/while/body/eval_jaxpr/rgw,wd->rgd/dot_general | solution.py:72
  211.3 0.2 and_and_fusion.2
  211.5 2.1 fusion.43
  213.6 1.0 fusion.44
  214.6 2.6 %fusion.45 = bf16[8,128,8,128]{3,1,2,0:T(8,128)(2,1)} fusion(bf16[8,128,8,128]{3,1,2,0:T(8,128)(2,1)} %get-tuple-element.200, s32[]{:T(128)S(6)} %copy.43, f32[128,8,1152]{2,0,1:T(8,128)S(1)} %get-tuple-element.186, f32[128,8]{0,1:T(8,128)S(1)} %get-tuple-element.187, bf16[8,1152,128]{1,2,0:T(8,128)(2,1)} %get-tuple-element.214, ...), kind=kOutput, calls=%fused_computation.11.clone.1 | convolution fusion | flops 304611328 | bytes 5284864 | tf_op jit(solution)/shard_map/while/body/eval_jaxpr/rgw,wd->rgd/dot_general | solution.py:72
  217.2 2.9 %copy.22 = bf16[128,8,8,128]{3,2,1,0:T(8,128)(2,1)S(1)} copy(bf16[128,8,8,128]{3,0,2,1:T(8,128)(2,1)} %bitcast.52) | data formatting | bytes 4194304 | tf_op jit(solution)/shard_map/transpose | solution.py:76
  220.1 2.3 %broadcast_in_dim_reshape.3 = bf16[1,128,8192]{2,1,0:T(8,128)(2,1)} reshape(bf16[128,8,8,128]{3,2,1,0:T(8,128)(2,1)S(1)} %copy.22) | data formatting | bytes 4194304 | tf_op jit(solution)/shard_map/broadcast_in_dim;reshape | solution.py:96
  (28 shorter events, 1.5 us)
Async XLA Ops:
  14.6 32.5 %collective-permute-start = (bf16[2,128,1024]{1,2,0:T(8,128)(2,1)S(1)}, bf16[2,128,1024]{1,2,0:T(8,128)(2,1)}, u32[]{:S(2)}, u32[]{:S(2)}) collective-permute-start(bf16[2,128,1024]{1,2,0:T(8,128)(2,1)S(1)} %all_gather.3), channel_id=1, source_target_pairs={{0,8},{1,9},{2,10},{3,11},{4,12},{5,13},{6,14},{7,15},{8,16},{9,17... | collective-permute-start | bytes 1572872 | tf_op jit(solution)/shard_map/ppermute | solution.py:17
  15.9 50.9 %collective-permute-start.1 = (bf16[2,128,1024]{1,2,0:T(8,128)(2,1)S(1)}, bf16[2,128,1024]{1,2,0:T(8,128)(2,1)S(1)}, u32[]{:S(2)}, u32[]{:S(2)}) collective-permute-start(bf16[2,128,1024]{1,2,0:T(8,128)(2,1)S(1)} %all_gather.3), channel_id=1, source_target_pairs={{0,7},{1,8},{2,9},{3,10},{4,11},{5,12},{6,13},{7,14},{8,15},{9,16}... | collective-permute-start | bytes 1572872 | tf_op jit(solution)/shard_map/ppermute | solution.py:17
  21.0 69.8 %collective-permute-start.2 = (bf16[2,128,1024]{1,2,0:T(8,128)(2,1)S(1)}, bf16[2,128,1024]{1,2,0:T(8,128)(2,1)S(1)}, u32[]{:S(2)}, u32[]{:S(2)}) collective-permute-start(bf16[2,128,1024]{1,2,0:T(8,128)(2,1)S(1)} %all_gather.3), channel_id=1, source_target_pairs={{0,6},{1,7},{2,8},{3,9},{4,10},{5,11},{6,12},{7,13},{8,14},{9,15},... | collective-permute-start | bytes 1572872 | tf_op jit(solution)/shard_map/ppermute | solution.py:17
  22.9 90.0 %collective-permute-start.3 = (bf16[2,128,1024]{1,2,0:T(8,128)(2,1)S(1)}, bf16[2,128,1024]{1,2,0:T(8,128)(2,1)S(1)}, u32[]{:S(2)}, u32[]{:S(2)}) collective-permute-start(bf16[2,128,1024]{1,2,0:T(8,128)(2,1)S(1)} %all_gather.3), channel_id=1, source_target_pairs={{0,5},{1,6},{2,7},{3,8},{4,9},{5,10},{6,11},{7,12},{8,13},{9,14},{... | collective-permute-start | bytes 1572872 | tf_op jit(solution)/shard_map/ppermute | solution.py:17
  24.9 88.2 %collective-permute-start.4 = (bf16[2,128,1024]{1,2,0:T(8,128)(2,1)S(1)}, bf16[2,128,1024]{1,2,0:T(8,128)(2,1)S(1)}, u32[]{:S(2)}, u32[]{:S(2)}) collective-permute-start(bf16[2,128,1024]{1,2,0:T(8,128)(2,1)S(1)} %all_gather.3), channel_id=1, source_target_pairs={{0,4},{1,5},{2,6},{3,7},{4,8},{5,9},{6,10},{7,11},{8,12},{9,13},{1... | collective-permute-start | bytes 1572872 | tf_op jit(solution)/shard_map/ppermute | solution.py:17
  29.5 4.6 %copy-start.1 = (f32[1,64]{1,0:T(1,128)S(1)}, f32[1,64]{1,0:T(1,128)}, u32[]{:S(2)}) copy-start(f32[1,64]{1,0:T(1,128)} %param.8) | copy-start | bytes 772
  29.6 4.6 %copy-start = (s32[16]{0:T(128)S(1)}, s32[16]{0:T(128)}, u32[]{:S(2)}) copy-start(s32[16]{0:T(128)} %param.9) | copy-start | bytes 196
  47.1 72.9 %collective-permute-start.5 = (bf16[2,128,1024]{1,2,0:T(8,128)(2,1)S(1)}, bf16[2,128,1024]{1,2,0:T(8,128)(2,1)S(1)}, u32[]{:S(2)}, u32[]{:S(2)}) collective-permute-start(bf16[2,128,1024]{1,2,0:T(8,128)(2,1)S(1)} %all_gather.3), channel_id=1, source_target_pairs={{0,3},{1,4},{2,5},{3,6},{4,7},{5,8},{6,9},{7,10},{8,11},{9,12},{10... | collective-permute-start | bytes 1572872 | tf_op jit(solution)/shard_map/ppermute | solution.py:17
  66.7 68.0 %collective-permute-start.6 = (bf16[2,128,1024]{1,2,0:T(8,128)(2,1)S(1)}, bf16[2,128,1024]{1,2,0:T(8,128)(2,1)S(1)}, u32[]{:S(2)}, u32[]{:S(2)}) collective-permute-start(bf16[2,128,1024]{1,2,0:T(8,128)(2,1)S(1)} %all_gather.3), channel_id=1, source_target_pairs={{0,2},{1,3},{2,4},{3,5},{4,6},{5,7},{6,8},{7,9},{8,10},{9,11},{10,... | collective-permute-start | bytes 1572872 | tf_op jit(solution)/shard_map/ppermute | solution.py:17
  90.8 75.9 %collective-permute-start.7 = (bf16[2,128,1024]{1,2,0:T(8,128)(2,1)S(1)}, bf16[2,128,1024]{1,2,0:T(8,128)(2,1)S(1)}, u32[]{:S(2)}, u32[]{:S(2)}) collective-permute-start(bf16[2,128,1024]{1,2,0:T(8,128)(2,1)S(1)} %all_gather.3), channel_id=1, source_target_pairs={{0,1},{1,2},{2,3},{3,4},{4,5},{5,6},{6,7},{7,8},{8,9},{9,10},{10,1... | collective-permute-start | bytes 1572872 | tf_op jit(solution)/shard_map/ppermute | solution.py:17
where the time goes:
time: 223 us; the launch traced here: 222 us
  waiting for transfers between devices  112 us (50%)
  matrix products  37.5 us (17%)
  other arithmetic  25.7 us (12%)
  starting transfers between devices  18.1 us (8%)
  local copies, waits for them, and re-layouts  15.5 us (7%)
  blocking collectives  13.6 us (6%)
    ppermute x8, waiting for transfers between devices, passed_along(): lax.ppermute(value, axis, [(source, source + steps) for source in range(f...  112 us
    dot_general x8, matrix products, per_group(): jnp.einsum('rgw,wd->rgd', weights, v_part, preferred_element_type=jnp.flo...  20.8 us
    ppermute x8, starting transfers between devices, passed_along(): lax.ppermute(value, axis, [(source, source + steps) for source in range(f...  18.1 us
    dot_general x8, matrix products, per_group(): jnp.einsum('rgd,wd->rgw', q_part, k_part, preferred_element_type=jnp.floa...  16.7 us
    all_gather x1, blocking collectives, on_device(): whole = lax.all_gather(keys_values, 'cand', axis=2, tiled=True)  13.6 us
    another operation x4, other arithmetic  9.14 us
    reduce_sum x8, other arithmetic, per_group(): total = jnp.sum(expw, axis=-1, keepdims=True)  8.08 us
    slice x1, local copies, waits for them, and re-layouts, rotate(): first_half = shaped[..., :half_dim]  4.58 us
  transfers between devices with their start and end apart: 8, of which 6 were waited for; matrix products, arithmetic and copies ran while one was open for 10% of the time, Pallas kernels for 0%

commit v1 on v0

--- a/solution.py
+++ b/solution.py
@@ -1,3 +1,4 @@
+import functools
 import math
 import jax
 import jax.numpy as jnp
@@ -9,6 +10,18 @@
 HD = 128
 SPAN = 8
 ROPE_BASE = 500000.0
+
+
+def time_slot(matrix, chip_axis, at_axis):
+    size_here = lax.axis_size(chip_axis)
+    sheets = list(map(lambda idx: size_here if idx == at_axis else 1, range(matrix.ndim)))
+    outer = lax.all_to_all(
+        jnp.tile(matrix, sheets), chip_axis, split_axis=at_axis, tiled=True, concat_axis=at_axis
+    )
+    return outer
+
+
+divide_the_rates = functools.partial(time_slot, chip_axis="cand", at_axis=2)
 
 
 def passed_along(value, axis, steps):
@@ -81,7 +94,7 @@
     device = lax.axis_index("doc")
     query_index = device * row_count + jnp.arange(row_count, dtype=jnp.int32)
     key_index = (device - SPAN) * row_count + jnp.arange((SPAN + 1) * row_count, dtype=jnp.int32)
-    whole = lax.all_gather(keys_values, "cand", axis=2, tiled=True)
+    whole = divide_the_rates(keys_values)
     pieces = []
     for distance in range(SPAN, 0, -1):
         pieces.append(passed_along(whole, "doc", distance))

time: 223 us -> 235 us (1.054)
  blocking collectives: 13.6 us -> 0 us
  waiting for transfers between devices: 112 us -> 121 us
  starting transfers between devices: 18.1 us -> 25.3 us
  local copies, waits for them, and re-layouts: 15.5 us -> 21.7 us
  other arithmetic: 25.7 us -> 28.5 us
    all_gather x1 -> x0, blocking collectives: 13.6 us -> none  [on_device(): whole = lax.all_gather(keys_values, 'cand', axis=2, tiled=True)]
    ppermute x8, waiting for transfers between devices: 112 us -> 121 us  [passed_along(): lax.ppermute(value, axis, [(source, source + steps) for source in range(f...]
    all_to_all x0 -> x1, starting transfers between devices: none -> 4.47 us  [time_slot(): lax.all_to_all(jnp.tile(matrix, sheets), chip_axis, split_axis=at_axis, t...]
    unnamed x14, local copies, waits for them, and re-layouts: 3.71 us -> 7.88 us
    ppermute x8, starting transfers between devices: 18.1 us -> 20.9 us  [passed_along(): lax.ppermute(value, axis, [(source, source + steps) for source in range(f...]
  transfers between devices with their start and end apart: 8 -> 9, of which waited for: 6 -> 7; matrix products, arithmetic and copies ran while one was open for 10% -> 12% of each run, Pallas kernels for 0% -> 0%
where the time goes in v1:
time: 235 us; the launch traced here: 234 us
  waiting for transfers between devices  121 us (51%)
  matrix products  37.5 us (16%)
  other arithmetic  28.5 us (12%)
  starting transfers between devices  25.3 us (11%)
  local copies, waits for them, and re-layouts  21.7 us (9%)
    ppermute x8, waiting for transfers between devices, passed_along(): lax.ppermute(value, axis, [(source, source + steps) for source in range(f...  121 us
    ppermute x8, starting transfers between devices, passed_along(): lax.ppermute(value, axis, [(source, source + steps) for source in range(f...  20.9 us
    dot_general x8, matrix products, per_group(): jnp.einsum('rgw,wd->rgd', weights, v_part, preferred_element_type=jnp.flo...  20.8 us
    dot_general x8, matrix products, per_group(): jnp.einsum('rgd,wd->rgw', q_part, k_part, preferred_element_type=jnp.floa...  16.7 us
    another operation x4, other arithmetic  10.5 us
    reduce_sum x8, other arithmetic, per_group(): total = jnp.sum(expw, axis=-1, keepdims=True)  8.08 us
    unnamed x14, local copies, waits for them, and re-layouts  7.88 us
  transfers between devices with their start and end apart: 9, of which 7 were waited for; matrix products, arithmetic and copies ran while one was open for 12% of the time, Pallas kernels for 0%

profile of v1, /device:TPU:448, one launch (start us, length us, event | category | flops | bytes accessed | tf_op | source)
XLA Modules:
  0.0 234.0 jit_solution(4008718499883065123)
XLA Ops:
  0.0 1.0 copy.35
  1.0 1.1 tile.4
  2.1 4.5 %all-to-all-start = ((bf16[2,128,1024]{1,0,2:T(2,128)(2,1)}), bf16[2,128,1024]{1,0,2:T(2,128)(2,1)S(1)}, u32[]{:S(2)}, u32[]{:S(2)}) async-start(bf16[2,128,1024]{1,0,2:T(2,128)(2,1)} %bitcast.4), calls=%async_computation | async-start | bytes 1048576 | tf_op jit(solution)/shard_map/all_to_all | solution.py:18
  6.6 2.0 convert_bitcast_fusion
  8.6 0.7 copy.52
  9.3 4.6 %fusion.35 = (f32[128,64,64]{2,1,0:T(8,128)}, f32[128,64,64]{2,1,0:T(8,128)}) fusion(f32[128,64,128]{2,1,0:T(8,128)S(1)} %bitcast.49), kind=kLoop, calls=%fused_computation.60 | loop fusion | bytes 8388608 | tf_op jit(solution)/shard_map/slice | solution.py:52
  14.6 0.3 multiply_cosine_fusion.1
  14.9 9.7 %subtract_convert_fusion = (bf16[128,64,64]{2,0,1:T(8,128)(2,1)S(1)}, bf16[128,64,64]{2,0,1:T(8,128)(2,1)}) fusion(f32[128,64,64]{2,1,0:T(8,128)} %get-tuple-element.126, f32[128,64,64]{2,1,0:T(8,128)} %get-tuple-element.125, f32[128,64]{1,0:T(8,128)S(1)} %get-tuple-element.130, f32[128,64]{1,0:T(8,128)S(1)} %get-tuple-element.129), kind=kLoop, calls=%fused_computation.23 | loop fusion | flops 4194304 | bytes 6356992 | tf_op jit(solution)/shard_map/convert.4
  24.6 0.9 copy.36
  25.4 1.3 collective-permute-start
  26.7 5.1 %collective-permute-start.1 = (bf16[2,128,1024]{1,2,0:T(8,128)(2,1)}, bf16[2,128,1024]{1,2,0:T(8,128)(2,1)}, u32[]{:S(2)}, u32[]{:S(2)}) collective-permute-start(bf16[2,128,1024]{1,2,0:T(8,128)(2,1)} %copy.36), channel_id=1, source_target_pairs={{0,7},{1,8},{2,9},{3,10},{4,11},{5,12},{6,13},{7,14},{8,15},{9,16}... | collective-permute-start | bytes 1572872 | tf_op jit(solution)/shard_map/ppermute | solution.py:30
  31.8 1.1 multiply_cosine_fusion
  32.9 1.9 collective-permute-start.2
  34.9 1.9 collective-permute-start.3
  36.8 1.9 collective-permute-start.4
  38.7 4.1 %pad_maximum_fusion = bf16[128,64,128]{2,0,1:T(8,128)(2,1)} fusion(bf16[128,64,64]{2,0,1:T(8,128)(2,1)} %get-tuple-element.120, bf16[128,64,64]{2,0,1:T(8,128)(2,1)S(1)} %get-tuple-element.119), kind=kLoop, calls=%fused_computation.27 | loop fusion | flops 4194304 | bytes 4194304 | tf_op jit(solution)/shard_map/concatenate | solution.py:54
  42.8 2.1 collective-permute-done
  44.9 4.7 %collective-permute-start.5 = (bf16[2,128,1024]{1,2,0:T(8,128)(2,1)}, bf16[2,128,1024]{1,2,0:T(8,128)(2,1)S(1)}, u32[]{:S(2)}, u32[]{:S(2)}) collective-permute-start(bf16[2,128,1024]{1,2,0:T(8,128)(2,1)} %copy.36), channel_id=1, source_target_pairs={{0,3},{1,4},{2,5},{3,6},{4,7},{5,8},{6,9},{7,10},{8,11},{9,12},{10... | collective-permute-start | bytes 1572872 | tf_op jit(solution)/shard_map/ppermute | solution.py:30
  49.6 1.1 constant_dynamic-update-slice_fusion.8
  50.7 27.1 %collective-permute-done.1 = bf16[2,128,1024]{1,2,0:T(8,128)(2,1)} collective-permute-done((bf16[2,128,1024]{1,2,0:T(8,128)(2,1)}, bf16[2,128,1024]{1,2,0:T(8,128)(2,1)}, u32[]{:S(2)}, u32[]{:S(2)}) %collective-permute-start.1) | collective-permute-done | bytes 524320 | tf_op jit(solution)/shard_map/ppermute | solution.py:30
  77.9 2.1 collective-permute-start.6
  80.0 1.2 constant_dynamic-update-slice_fusion.7
  81.2 20.7 %collective-permute-done.2 = bf16[2,128,1024]{1,2,0:T(8,128)(2,1)} collective-permute-done((bf16[2,128,1024]{1,2,0:T(8,128)(2,1)}, bf16[2,128,1024]{1,2,0:T(8,128)(2,1)}, u32[]{:S(2)}, u32[]{:S(2)}) %collective-permute-start.2) | collective-permute-done | bytes 524320 | tf_op jit(solution)/shard_map/ppermute | solution.py:30
  101.9 1.9 collective-permute-start.7
  103.8 1.2 constant_dynamic-update-slice_fusion.6
  105.0 19.1 %collective-permute-done.3 = bf16[2,128,1024]{1,2,0:T(8,128)(2,1)} collective-permute-done((bf16[2,128,1024]{1,2,0:T(8,128)(2,1)}, bf16[2,128,1024]{1,2,0:T(8,128)(2,1)}, u32[]{:S(2)}, u32[]{:S(2)}) %collective-permute-start.3) | collective-permute-done | bytes 524320 | tf_op jit(solution)/shard_map/ppermute | solution.py:30
  124.1 1.2 constant_dynamic-update-slice_fusion.5
  125.3 1.2 constant_dynamic-update-slice_fusion.4
  126.5 5.0 %collective-permute-done.5 = bf16[2,128,1024]{1,2,0:T(8,128)(2,1)S(1)} collective-permute-done((bf16[2,128,1024]{1,2,0:T(8,128)(2,1)}, bf16[2,128,1024]{1,2,0:T(8,128)(2,1)S(1)}, u32[]{:S(2)}, u32[]{:S(2)}) %collective-permute-start.5) | collective-permute-done | bytes 524320 | tf_op jit(solution)/shard_map/ppermute | solution.py:30
  131.5 14.4 %collective-permute-done.6 = bf16[2,128,1024]{1,2,0:T(8,128)(2,1)S(1)} collective-permute-done((bf16[2,128,1024]{1,2,0:T(8,128)(2,1)}, bf16[2,128,1024]{1,2,0:T(8,128)(2,1)S(1)}, u32[]{:S(2)}, u32[]{:S(2)}) %collective-permute-start.6) | collective-permute-done | bytes 524320 | tf_op jit(solution)/shard_map/ppermute | solution.py:30
  146.1 32.1 %collective-permute-done.7 = bf16[2,128,1024]{1,2,0:T(8,128)(2,1)S(1)} collective-permute-done((bf16[2,128,1024]{1,2,0:T(8,128)(2,1)}, bf16[2,128,1024]{1,2,0:T(8,128)(2,1)S(1)}, u32[]{:S(2)}, u32[]{:S(2)}) %collective-permute-start.7) | collective-permute-done | bytes 524320 | tf_op jit(solution)/shard_map/ppermute | solution.py:30
  178.5 1.8 fusion.34
  180.3 0.3 convert.18
  180.6 0.6 subtract_convert_fusion.1
  181.2 0.2 maximum_bitcast_fusion
  181.5 47.3 %while.11 = (s32[]{:T(128)}, bf16[8,128,8,128]{3,1,2,0:T(8,128)(2,1)}, bf16[8,128,8,128]{3,1,2,0:T(8,128)(2,1)}, bf16[8,1152,128]{1,2,0:T(8,128)(2,1)S(1)}, bf16...) while((s32[]{:T(128)}, ...), condition=%wide.region_8.9_spmd.clone, body=%wide.region_5.8_spmd.clone.sunk | while | flops 613087232 | bytes 15598837 | solution.py:88
  181.5 0.2 and_and_fusion.2
  181.7 2.1 fusion.43
  183.8 1.0 fusion.44
  184.8 2.6 %fusion.45 = bf16[8,128,8,128]{3,1,2,0:T(8,128)(2,1)} fusion(bf16[8,128,8,128]{3,1,2,0:T(8,128)(2,1)} %get-tuple-element.210, s32[]{:T(128)S(6)} %copy.69, f32[128,8,1152]{2,0,1:T(8,128)S(1)} %get-tuple-element.196, f32[128,8]{0,1:T(8,128)S(1)} %get-tuple-element.197, bf16[8,1152,128]{1,2,0:T(8,128)(2,1)} %get-tuple-element.224, ...), kind=kOutput, calls=%fused_computation.11.clone.1 | convolution fusion | flops 304611328 | bytes 5284864 | tf_op jit(solution)/shard_map/while/body/eval_jaxpr/rgw,wd->rgd/dot_general | solution.py:85
  187.4 0.2 and_and_fusion.2
  187.6 2.1 fusion.43
  189.7 1.0 fusion.44
  190.7 2.6 %fusion.45 = bf16[8,128,8,128]{3,1,2,0:T(8,128)(2,1)} fusion(bf16[8,128,8,128]{3,1,2,0:T(8,128)(2,1)} %get-tuple-element.210, s32[]{:T(128)S(6)} %copy.69, f32[128,8,1152]{2,0,1:T(8,128)S(1)} %get-tuple-element.196, f32[128,8]{0,1:T(8,128)S(1)} %get-tuple-element.197, bf16[8,1152,128]{1,2,0:T(8,128)(2,1)} %get-tuple-element.224, ...), kind=kOutput, calls=%fused_computation.11.clone.1 | convolution fusion | flops 304611328 | bytes 5284864 | tf_op jit(solution)/shard_map/while/body/eval_jaxpr/rgw,wd->rgd/dot_general | solution.py:85
  193.5 2.1 fusion.43
  195.6 1.0 fusion.44
  196.6 2.6 %fusion.45 = bf16[8,128,8,128]{3,1,2,0:T(8,128)(2,1)} fusion(bf16[8,128,8,128]{3,1,2,0:T(8,128)(2,1)} %get-tuple-element.210, s32[]{:T(128)S(6)} %copy.69, f32[128,8,1152]{2,0,1:T(8,128)S(1)} %get-tuple-element.196, f32[128,8]{0,1:T(8,128)S(1)} %get-tuple-element.197, bf16[8,1152,128]{1,2,0:T(8,128)(2,1)} %get-tuple-element.224, ...), kind=kOutput, calls=%fused_computation.11.clone.1 | convolution fusion | flops 304611328 | bytes 5284864 | tf_op jit(solution)/shard_map/while/body/eval_jaxpr/rgw,wd->rgd/dot_general | solution.py:85
  199.4 2.1 fusion.43
  201.5 1.0 fusion.44
  202.5 2.6 %fusion.45 = bf16[8,128,8,128]{3,1,2,0:T(8,128)(2,1)} fusion(bf16[8,128,8,128]{3,1,2,0:T(8,128)(2,1)} %get-tuple-element.210, s32[]{:T(128)S(6)} %copy.69, f32[128,8,1152]{2,0,1:T(8,128)S(1)} %get-tuple-element.196, f32[128,8]{0,1:T(8,128)S(1)} %get-tuple-element.197, bf16[8,1152,128]{1,2,0:T(8,128)(2,1)} %get-tuple-element.224, ...), kind=kOutput, calls=%fused_computation.11.clone.1 | convolution fusion | flops 304611328 | bytes 5284864 | tf_op jit(solution)/shard_map/while/body/eval_jaxpr/rgw,wd->rgd/dot_general | solution.py:85
  205.3 2.1 fusion.43
  207.4 1.0 fusion.44
  208.4 2.6 %fusion.45 = bf16[8,128,8,128]{3,1,2,0:T(8,128)(2,1)} fusion(bf16[8,128,8,128]{3,1,2,0:T(8,128)(2,1)} %get-tuple-element.210, s32[]{:T(128)S(6)} %copy.69, f32[128,8,1152]{2,0,1:T(8,128)S(1)} %get-tuple-element.196, f32[128,8]{0,1:T(8,128)S(1)} %get-tuple-element.197, bf16[8,1152,128]{1,2,0:T(8,128)(2,1)} %get-tuple-element.224, ...), kind=kOutput, calls=%fused_computation.11.clone.1 | convolution fusion | flops 304611328 | bytes 5284864 | tf_op jit(solution)/shard_map/while/body/eval_jaxpr/rgw,wd->rgd/dot_general | solution.py:85
  211.2 2.1 fusion.43
  213.3 1.0 fusion.44
  214.3 2.6 %fusion.45 = bf16[8,128,8,128]{3,1,2,0:T(8,128)(2,1)} fusion(bf16[8,128,8,128]{3,1,2,0:T(8,128)(2,1)} %get-tuple-element.210, s32[]{:T(128)S(6)} %copy.69, f32[128,8,1152]{2,0,1:T(8,128)S(1)} %get-tuple-element.196, f32[128,8]{0,1:T(8,128)S(1)} %get-tuple-element.197, bf16[8,1152,128]{1,2,0:T(8,128)(2,1)} %get-tuple-element.224, ...), kind=kOutput, calls=%fused_computation.11.clone.1 | convolution fusion | flops 304611328 | bytes 5284864 | tf_op jit(solution)/shard_map/while/body/eval_jaxpr/rgw,wd->rgd/dot_general | solution.py:85
  217.1 2.1 fusion.43
  219.2 1.0 fusion.44
  220.2 2.6 %fusion.45 = bf16[8,128,8,128]{3,1,2,0:T(8,128)(2,1)} fusion(bf16[8,128,8,128]{3,1,2,0:T(8,128)(2,1)} %get-tuple-element.210, s32[]{:T(128)S(6)} %copy.69, f32[128,8,1152]{2,0,1:T(8,128)S(1)} %get-tuple-element.196, f32[128,8]{0,1:T(8,128)S(1)} %get-tuple-element.197, bf16[8,1152,128]{1,2,0:T(8,128)(2,1)} %get-tuple-element.224, ...), kind=kOutput, calls=%fused_computation.11.clone.1 | convolution fusion | flops 304611328 | bytes 5284864 | tf_op jit(solution)/shard_map/while/body/eval_jaxpr/rgw,wd->rgd/dot_general | solution.py:85
  223.0 2.1 fusion.43
  225.1 1.0 fusion.44
  226.1 2.6 %fusion.45 = bf16[8,128,8,128]{3,1,2,0:T(8,128)(2,1)} fusion(bf16[8,128,8,128]{3,1,2,0:T(8,128)(2,1)} %get-tuple-element.210, s32[]{:T(128)S(6)} %copy.69, f32[128,8,1152]{2,0,1:T(8,128)S(1)} %get-tuple-element.196, f32[128,8]{0,1:T(8,128)S(1)} %get-tuple-element.197, bf16[8,1152,128]{1,2,0:T(8,128)(2,1)} %get-tuple-element.224, ...), kind=kOutput, calls=%fused_computation.11.clone.1 | convolution fusion | flops 304611328 | bytes 5284864 | tf_op jit(solution)/shard_map/while/body/eval_jaxpr/rgw,wd->rgd/dot_general | solution.py:85
  228.7 2.9 %copy.47 = bf16[128,8,8,128]{3,2,1,0:T(8,128)(2,1)S(1)} copy(bf16[128,8,8,128]{3,0,2,1:T(8,128)(2,1)} %bitcast.53) | data formatting | bytes 4194304 | tf_op jit(solution)/shard_map/transpose | solution.py:89
  231.7 2.3 broadcast_in_dim_reshape.3
  (31 shorter events, 2.4 us)
Async XLA Ops:
  2.1 22.5 %all-to-all-start = ((bf16[2,128,1024]{1,0,2:T(2,128)(2,1)}), bf16[2,128,1024]{1,0,2:T(2,128)(2,1)S(1)}, u32[]{:S(2)}, u32[]{:S(2)}) async-start(bf16[2,128,1024]{1,0,2:T(2,128)(2,1)} %bitcast.4), calls=%async_computation | async-start | bytes 1048576 | tf_op jit(solution)/shard_map/all_to_all | solution.py:18
  9.3 4.6 %copy-start.1 = (f32[1,64]{1,0:T(1,128)S(1)}, f32[1,64]{1,0:T(1,128)}, u32[]{:S(2)}) copy-start(f32[1,64]{1,0:T(1,128)} %param.8) | copy-start | bytes 772
  9.3 4.6 %copy-start = (s32[16]{0:T(128)S(1)}, s32[16]{0:T(128)}, u32[]{:S(2)}) copy-start(s32[16]{0:T(128)} %param.9) | copy-start | bytes 196
  25.4 19.5 %collective-permute-start = (bf16[2,128,1024]{1,2,0:T(8,128)(2,1)}, bf16[2,128,1024]{1,2,0:T(8,128)(2,1)}, u32[]{:S(2)}, u32[]{:S(2)}) collective-permute-start(bf16[2,128,1024]{1,2,0:T(8,128)(2,1)} %copy.36), channel_id=1, source_target_pairs={{0,8},{1,9},{2,10},{3,11},{4,12},{5,13},{6,14},{7,15},{8,16},{9,17... | collective-permute-start | bytes 1572872 | tf_op jit(solution)/shard_map/ppermute | solution.py:30
  26.7 51.2 %collective-permute-start.1 = (bf16[2,128,1024]{1,2,0:T(8,128)(2,1)}, bf16[2,128,1024]{1,2,0:T(8,128)(2,1)}, u32[]{:S(2)}, u32[]{:S(2)}) collective-permute-start(bf16[2,128,1024]{1,2,0:T(8,128)(2,1)} %copy.36), channel_id=1, source_target_pairs={{0,7},{1,8},{2,9},{3,10},{4,11},{5,12},{6,13},{7,14},{8,15},{9,16}... | collective-permute-start | bytes 1572872 | tf_op jit(solution)/shard_map/ppermute | solution.py:30
  32.9 69.0 %collective-permute-start.2 = (bf16[2,128,1024]{1,2,0:T(8,128)(2,1)}, bf16[2,128,1024]{1,2,0:T(8,128)(2,1)}, u32[]{:S(2)}, u32[]{:S(2)}) collective-permute-start(bf16[2,128,1024]{1,2,0:T(8,128)(2,1)} %copy.36), channel_id=1, source_target_pairs={{0,6},{1,7},{2,8},{3,9},{4,10},{5,11},{6,12},{7,13},{8,14},{9,15},... | collective-permute-start | bytes 1572872 | tf_op jit(solution)/shard_map/ppermute | solution.py:30
  34.9 89.2 %collective-permute-start.3 = (bf16[2,128,1024]{1,2,0:T(8,128)(2,1)}, bf16[2,128,1024]{1,2,0:T(8,128)(2,1)}, u32[]{:S(2)}, u32[]{:S(2)}) collective-permute-start(bf16[2,128,1024]{1,2,0:T(8,128)(2,1)} %copy.36), channel_id=1, source_target_pairs={{0,5},{1,6},{2,7},{3,8},{4,9},{5,10},{6,11},{7,12},{8,13},{9,14},{... | collective-permute-start | bytes 1572872 | tf_op jit(solution)/shard_map/ppermute | solution.py:30
  36.8 88.5 %collective-permute-start.4 = (bf16[2,128,1024]{1,2,0:T(8,128)(2,1)}, bf16[2,128,1024]{1,2,0:T(8,128)(2,1)}, u32[]{:S(2)}, u32[]{:S(2)}) collective-permute-start(bf16[2,128,1024]{1,2,0:T(8,128)(2,1)} %copy.36), channel_id=1, source_target_pairs={{0,4},{1,5},{2,6},{3,7},{4,8},{5,9},{6,10},{7,11},{8,12},{9,13},{1... | collective-permute-start | bytes 1572872 | tf_op jit(solution)/shard_map/ppermute | solution.py:30
  44.9 86.5 %collective-permute-start.5 = (bf16[2,128,1024]{1,2,0:T(8,128)(2,1)}, bf16[2,128,1024]{1,2,0:T(8,128)(2,1)S(1)}, u32[]{:S(2)}, u32[]{:S(2)}) collective-permute-start(bf16[2,128,1024]{1,2,0:T(8,128)(2,1)} %copy.36), channel_id=1, source_target_pairs={{0,3},{1,4},{2,5},{3,6},{4,7},{5,8},{6,9},{7,10},{8,11},{9,12},{10... | collective-permute-start | bytes 1572872 | tf_op jit(solution)/shard_map/ppermute | solution.py:30
  77.9 68.1 %collective-permute-start.6 = (bf16[2,128,1024]{1,2,0:T(8,128)(2,1)}, bf16[2,128,1024]{1,2,0:T(8,128)(2,1)S(1)}, u32[]{:S(2)}, u32[]{:S(2)}) collective-permute-start(bf16[2,128,1024]{1,2,0:T(8,128)(2,1)} %copy.36), channel_id=1, source_target_pairs={{0,2},{1,3},{2,4},{3,5},{4,6},{5,7},{6,8},{7,9},{8,10},{9,11},{10,... | collective-permute-start | bytes 1572872 | tf_op jit(solution)/shard_map/ppermute | solution.py:30
  101.9 76.3 %collective-permute-start.7 = (bf16[2,128,1024]{1,2,0:T(8,128)(2,1)}, bf16[2,128,1024]{1,2,0:T(8,128)(2,1)S(1)}, u32[]{:S(2)}, u32[]{:S(2)}) collective-permute-start(bf16[2,128,1024]{1,2,0:T(8,128)(2,1)} %copy.36), channel_id=1, source_target_pairs={{0,1},{1,2},{2,3},{3,4},{4,5},{5,6},{6,7},{7,8},{8,9},{9,10},{10,1... | collective-permute-start | bytes 1572872 | tf_op jit(solution)/shard_map/ppermute | solution.py:30
